TPU v7x, 32 devices: a whole 2x2x4 slice. The times are simulated.
32 devices in a mesh: parts: 2 (over y), chain: 4 (over x, core), group: 4 (over z).
Axes of the slice: x: 2, y: 2, z: 4, core: 2. Of those that a mesh axis runs over, the one named last changes fastest.
Arguments:
- rhs: float32 [8, 5, 64, 64], P(('parts', 'chain'), None, None, 'group'), parts along dimension 0, may hold values from -6 to 6
- inv_block: float32 [8, 64, 320, 320], P(('parts', 'chain'), 'group'), parts along dimension 0, may hold values from -0.3125 to 0.3125
- flux_jac: float32 [8, 3, 5, 5, 64], P(('parts', 'chain'), None, None, None, 'group'), parts along dimension 0, may hold values from -2.5 to 2.5
- up_elem: int32 [8, 3, 64], P(('parts', 'chain'), None, 'group'), parts along dimension 0, may hold values from 0 to 63, each once within a row
- lift: float32 [3, 64, 16], replicated, may hold values from -0.875 to 0.875
Outputs:
- solution: float32 [8, 5, 64, 64], P(('parts', 'chain'), None, None, 'group'), parts along dimension 0
There are 2 independent parts, one for each index of `parts`. A program takes and returns all parts, laid end to end along the dimension named above; an argument that names none is the same for every part. Nothing has to cross between parts.
Inputs may be any that keep to these rules, and one draw needn't show every extreme that they name: For every section s and face k, up_elem[s, k, :] names each of the 64 elements once; row s = 0 is not read.
All inputs are finite; a program needn't handle non-finite values.
Results may differ from a plain program's by a relative error of at most 0.02.
Values may be sent and summed in bfloat16 or wider, within the bound.
No kernel may reach another device: no remote copies, remote signals or barrier semaphores. Data moves between devices by JAX's collectives and lax.ppermute only.
A program may use at most 64 MiB of HBM per device.

v0:
```python
import jax
import jax.numpy as jnp
from jax import lax
from jax.sharding import PartitionSpec as P

VARS = 5
NP = 4
NODES = 64
FACE = 16
HIGH = lax.Precision.HIGHEST


def passed_along(value, axis, steps):
    count = lax.axis_size(axis)
    initial, last = (max(0, -steps), min(count, count - steps))
    return lax.ppermute(value, axis, [(source, source + steps) for source in range(initial, last)])


def face_traces(solved):
    elements = solved.shape[-1]
    cube = solved.reshape(VARS, NP, NP, NP, elements)
    first = cube[:, NP - 1, :, :, :].reshape(VARS, FACE, elements)
    second = cube[:, :, NP - 1, :, :].reshape(VARS, FACE, elements)
    third = cube[:, :, :, NP - 1, :].reshape(VARS, FACE, elements)
    return jnp.stack([first, second, third]).astype(jnp.bfloat16)


def solve_section(rhs_s, inv_s, jac_s, up_s, prev_full, lift):
    elements = rhs_s.shape[-1]
    picked = jnp.stack([jnp.take(prev_full[k], up_s[k], axis=2) for k in range(3)])
    upstream = picked.astype(jnp.float32)
    mixed = jnp.einsum("kwve,kvfe->kwfe", jac_s, upstream, precision=HIGH)
    coupling = jnp.einsum("kif,kwfe->wie", lift, mixed, precision=HIGH)
    flat = (rhs_s - coupling).reshape(VARS * NODES, elements)
    result = jnp.einsum("eij,je->ie", inv_s, flat, precision=HIGH)
    return result.reshape(VARS, NODES, elements)


def body(rhs, inv_block, flux_jac, up_elem, lift):
    local = rhs.shape[3]
    chains = lax.axis_size("chain")

    def chain_step(turn, carry):
        last_traces, solved_all = carry
        previous = passed_along(last_traces, "chain", 1)
        full_front = lax.all_gather(previous, "group", axis=3, tiled=True)
        solved = solve_section(rhs[0], inv_block[0], flux_jac[0], up_elem[0], full_front, lift)
        solved_list = [solved]
        previous = face_traces(solved)
        return (previous, jnp.stack(solved_list))

    start = (jnp.zeros((3, VARS, FACE, local), jnp.bfloat16), jnp.zeros(rhs.shape, jnp.float32))
    ended, solution = lax.fori_loop(0, chains, chain_step, start)
    return solution


def solution(mesh):
    return jax.shard_map(
        body,
        mesh=mesh,
        in_specs=(
            P(("parts", "chain"), None, None, "group"),
            P(("parts", "chain"), "group", None, None),
            P(("parts", "chain"), None, None, None, "group"),
            P(("parts", "chain"), None, "group"),
            P(),
        ),
        out_specs=P(("parts", "chain"), None, None, "group"),
        check_vma=False,
    )
```

profile of v0, /device:TPU:6, one launch (start us, length us, event | category | flops | bytes accessed | tf_op | source)
XLA Modules:
  0.0 141.2 jit_solution(16525215014715003966)
XLA Ops:
  0.0 0.8 copy.30
  0.8 0.7 copy.29
  1.5 138.2 %while.12 = (s32[]{:T(128)}, bf16[3,5,16,16]{3,2,1,0:T(8,128)(2,1)S(1)}, f32[1,5,64,16]{2,1,3,0:T(8,128)}, f32[1,5,64,16]{2,3,1,0:T(8,128)}, s32[1,3,16]{2,1,0:T...) while((s32[]{:T(128)}, ...), condition=%wide.region_1.3_spmd, body=%wide.region_0.2_spmd.sunk | while | flops 22868000 | bytes 7120933 | solution.py:53
  1.5 0.1 copy.50
  1.6 1.9 %collective-permute-start = (bf16[3,5,16,16]{2,1,3,0:T(8,128)(2,1)S(1)}, bf16[3,5,16,16]{2,1,3,0:T(8,128)(2,1)S(1)}, u32[]{:S(2)}, u32[]{:S(2)}) collective-permute-start(bf16[3,5,16,16]{2,1,3,0:T(8,128)(2,1)S(1)} %copy.50), channel_id=1, source_target_pairs={{0,4},{4,8},{8,12},{1,5},{5,9},{9,13},{2,6},{6,10},{10,14},{3,7},{... | collective-permute-start | bytes 23048 | tf_op jit(solution)/shard_map/while/body/eval_jaxpr/ppermute | solution.py:16
  3.6 0.2 copy.49
  3.8 3.8 %collective-permute-done = bf16[3,5,16,16]{2,1,3,0:T(8,128)(2,1)S(1)} collective-permute-done((bf16[3,5,16,16]{2,1,3,0:T(8,128)(2,1)S(1)}, bf16[3,5,16,16]{2,1,3,0:T(8,128)(2,1)S(1)}, u32[]{:S(2)}, u32[]{:S(2)}) %collective-permute-start) | collective-permute-done | bytes 7712 | tf_op jit(solution)/shard_map/while/body/eval_jaxpr/ppermute | solution.py:16
  7.6 15.3 %all_gather.4 = bf16[3,5,16,64]{2,1,3,0:T(8,128)(2,1)S(1)} all-gather(bf16[3,5,16,16]{2,1,3,0:T(8,128)(2,1)S(1)} %collective-permute-done), channel_id=1, replica_groups=mesh['parts'=2,'chain'=4,'group'=4] {'group'}, dimensions={3}, use_global_device_ids=true | all-gather | bytes 38400 | tf_op jit(solution)/shard_map/while/body/eval_jaxpr/all_gather | solution.py:46
  23.0 0.6 gather_fusion.1
  23.6 0.6 gather_fusion
  24.1 0.6 gather_fusion.2
  24.8 0.1 select_bitcast_fusion.5
  24.9 0.3 convolution_bitcast_fusion.3
  25.2 1.1 fusion.27
  26.3 0.1 reshape.74
  26.4 9.1 %fusion.28 = f32[16,1,320]{2,1,0:T(1,128)S(1)} fusion(f32[320,16,1]{0,2,1:T(1,128)S(1)} %reshape.74, f32[1,16,320,320]{3,2,1,0:T(8,128)} %get-tuple-element.205), kind=kOutput, calls=%fused_computation.3.clone.1 | convolution fusion | flops 19660800 | bytes 6594560 | tf_op jit(solution)/shard_map/while/body/eval_jaxpr/eij,je->ie/dot_general | solution.py:35
  35.5 0.1 copy.52
  35.8 0.7 reshape.75
  36.5 0.1 copy.50
  36.7 1.9 %collective-permute-start = (bf16[3,5,16,16]{2,1,3,0:T(8,128)(2,1)S(1)}, bf16[3,5,16,16]{2,1,3,0:T(8,128)(2,1)S(1)}, u32[]{:S(2)}, u32[]{:S(2)}) collective-permute-start(bf16[3,5,16,16]{2,1,3,0:T(8,128)(2,1)S(1)} %copy.50), channel_id=1, source_target_pairs={{0,4},{4,8},{8,12},{1,5},{5,9},{9,13},{2,6},{6,10},{10,14},{3,7},{... | collective-permute-start | bytes 23048 | tf_op jit(solution)/shard_map/while/body/eval_jaxpr/ppermute | solution.py:16
  38.7 0.2 copy.49
  38.8 3.8 %collective-permute-done = bf16[3,5,16,16]{2,1,3,0:T(8,128)(2,1)S(1)} collective-permute-done((bf16[3,5,16,16]{2,1,3,0:T(8,128)(2,1)S(1)}, bf16[3,5,16,16]{2,1,3,0:T(8,128)(2,1)S(1)}, u32[]{:S(2)}, u32[]{:S(2)}) %collective-permute-start) | collective-permute-done | bytes 7712 | tf_op jit(solution)/shard_map/while/body/eval_jaxpr/ppermute | solution.py:16
  42.6 15.1 %all_gather.4 = bf16[3,5,16,64]{2,1,3,0:T(8,128)(2,1)S(1)} all-gather(bf16[3,5,16,16]{2,1,3,0:T(8,128)(2,1)S(1)} %collective-permute-done), channel_id=1, replica_groups=mesh['parts'=2,'chain'=4,'group'=4] {'group'}, dimensions={3}, use_global_device_ids=true | all-gather | bytes 38400 | tf_op jit(solution)/shard_map/while/body/eval_jaxpr/all_gather | solution.py:46
  57.8 0.6 gather_fusion.1
  58.4 0.6 gather_fusion
  59.0 0.6 gather_fusion.2
  59.6 0.1 select_bitcast_fusion.5
  59.7 0.3 convolution_bitcast_fusion.3
  60.1 1.1 fusion.27
  61.2 0.1 reshape.74
  61.2 9.1 %fusion.28 = f32[16,1,320]{2,1,0:T(1,128)S(1)} fusion(f32[320,16,1]{0,2,1:T(1,128)S(1)} %reshape.74, f32[1,16,320,320]{3,2,1,0:T(8,128)} %get-tuple-element.205), kind=kOutput, calls=%fused_computation.3.clone.1 | convolution fusion | flops 19660800 | bytes 6594560 | tf_op jit(solution)/shard_map/while/body/eval_jaxpr/eij,je->ie/dot_general | solution.py:35
  70.4 0.1 copy.52
  70.6 0.7 reshape.75
  71.4 0.1 copy.50
  71.5 1.9 %collective-permute-start = (bf16[3,5,16,16]{2,1,3,0:T(8,128)(2,1)S(1)}, bf16[3,5,16,16]{2,1,3,0:T(8,128)(2,1)S(1)}, u32[]{:S(2)}, u32[]{:S(2)}) collective-permute-start(bf16[3,5,16,16]{2,1,3,0:T(8,128)(2,1)S(1)} %copy.50), channel_id=1, source_target_pairs={{0,4},{4,8},{8,12},{1,5},{5,9},{9,13},{2,6},{6,10},{10,14},{3,7},{... | collective-permute-start | bytes 23048 | tf_op jit(solution)/shard_map/while/body/eval_jaxpr/ppermute | solution.py:16
  73.5 0.2 copy.49
  73.7 3.8 %collective-permute-done = bf16[3,5,16,16]{2,1,3,0:T(8,128)(2,1)S(1)} collective-permute-done((bf16[3,5,16,16]{2,1,3,0:T(8,128)(2,1)S(1)}, bf16[3,5,16,16]{2,1,3,0:T(8,128)(2,1)S(1)}, u32[]{:S(2)}, u32[]{:S(2)}) %collective-permute-start) | collective-permute-done | bytes 7712 | tf_op jit(solution)/shard_map/while/body/eval_jaxpr/ppermute | solution.py:16
  77.4 14.5 %all_gather.4 = bf16[3,5,16,64]{2,1,3,0:T(8,128)(2,1)S(1)} all-gather(bf16[3,5,16,16]{2,1,3,0:T(8,128)(2,1)S(1)} %collective-permute-done), channel_id=1, replica_groups=mesh['parts'=2,'chain'=4,'group'=4] {'group'}, dimensions={3}, use_global_device_ids=true | all-gather | bytes 38400 | tf_op jit(solution)/shard_map/while/body/eval_jaxpr/all_gather | solution.py:46
  92.0 0.6 gather_fusion.1
  92.6 0.6 gather_fusion
  93.2 0.6 gather_fusion.2
  93.8 0.1 select_bitcast_fusion.5
  94.0 0.3 convolution_bitcast_fusion.3
  94.3 1.1 fusion.27
  95.4 0.1 reshape.74
  95.5 9.1 %fusion.28 = f32[16,1,320]{2,1,0:T(1,128)S(1)} fusion(f32[320,16,1]{0,2,1:T(1,128)S(1)} %reshape.74, f32[1,16,320,320]{3,2,1,0:T(8,128)} %get-tuple-element.205), kind=kOutput, calls=%fused_computation.3.clone.1 | convolution fusion | flops 19660800 | bytes 6594560 | tf_op jit(solution)/shard_map/while/body/eval_jaxpr/eij,je->ie/dot_general | solution.py:35
  104.6 0.1 copy.52
  104.9 0.7 reshape.75
  105.6 0.1 copy.50
  105.7 1.9 %collective-permute-start = (bf16[3,5,16,16]{2,1,3,0:T(8,128)(2,1)S(1)}, bf16[3,5,16,16]{2,1,3,0:T(8,128)(2,1)S(1)}, u32[]{:S(2)}, u32[]{:S(2)}) collective-permute-start(bf16[3,5,16,16]{2,1,3,0:T(8,128)(2,1)S(1)} %copy.50), channel_id=1, source_target_pairs={{0,4},{4,8},{8,12},{1,5},{5,9},{9,13},{2,6},{6,10},{10,14},{3,7},{... | collective-permute-start | bytes 23048 | tf_op jit(solution)/shard_map/while/body/eval_jaxpr/ppermute | solution.py:16
  107.7 0.2 copy.49
  107.9 3.8 %collective-permute-done = bf16[3,5,16,16]{2,1,3,0:T(8,128)(2,1)S(1)} collective-permute-done((bf16[3,5,16,16]{2,1,3,0:T(8,128)(2,1)S(1)}, bf16[3,5,16,16]{2,1,3,0:T(8,128)(2,1)S(1)}, u32[]{:S(2)}, u32[]{:S(2)}) %collective-permute-start) | collective-permute-done | bytes 7712 | tf_op jit(solution)/shard_map/while/body/eval_jaxpr/ppermute | solution.py:16
  111.7 14.4 %all_gather.4 = bf16[3,5,16,64]{2,1,3,0:T(8,128)(2,1)S(1)} all-gather(bf16[3,5,16,16]{2,1,3,0:T(8,128)(2,1)S(1)} %collective-permute-done), channel_id=1, replica_groups=mesh['parts'=2,'chain'=4,'group'=4] {'group'}, dimensions={3}, use_global_device_ids=true | all-gather | bytes 38400 | tf_op jit(solution)/shard_map/while/body/eval_jaxpr/all_gather | solution.py:46
  126.2 0.6 gather_fusion.1
  126.7 0.6 gather_fusion
  127.3 0.6 gather_fusion.2
  128.0 0.1 select_bitcast_fusion.5
  128.1 0.3 convolution_bitcast_fusion.3
  128.4 1.1 fusion.27
  129.5 0.1 reshape.74
  129.6 9.1 %fusion.28 = f32[16,1,320]{2,1,0:T(1,128)S(1)} fusion(f32[320,16,1]{0,2,1:T(1,128)S(1)} %reshape.74, f32[1,16,320,320]{3,2,1,0:T(8,128)} %get-tuple-element.205), kind=kOutput, calls=%fused_computation.3.clone.1 | convolution fusion | flops 19660800 | bytes 6594560 | tf_op jit(solution)/shard_map/while/body/eval_jaxpr/eij,je->ie/dot_general | solution.py:35
  138.7 0.1 copy.52
  139.0 0.7 reshape.75
  139.7 1.5 %copy.31 = f32[1,5,64,16]{2,3,1,0:T(8,128)} copy(f32[1,5,64,16]{2,1,3,0:T(8,128)} %get-tuple-element.47) | data formatting | bytes 40960 | tf_op jit(solution)/shard_map/while | solution.py:53
  (54 shorter events, 1.2 us)
Async XLA Ops:
  1.6 5.9 %collective-permute-start = (bf16[3,5,16,16]{2,1,3,0:T(8,128)(2,1)S(1)}, bf16[3,5,16,16]{2,1,3,0:T(8,128)(2,1)S(1)}, u32[]{:S(2)}, u32[]{:S(2)}) collective-permute-start(bf16[3,5,16,16]{2,1,3,0:T(8,128)(2,1)S(1)} %copy.50), channel_id=1, source_target_pairs={{0,4},{4,8},{8,12},{1,5},{5,9},{9,13},{2,6},{6,10},{10,14},{3,7},{... | collective-permute-start | bytes 23048 | tf_op jit(solution)/shard_map/while/body/eval_jaxpr/ppermute | solution.py:16
  36.7 5.9 %collective-permute-start = (bf16[3,5,16,16]{2,1,3,0:T(8,128)(2,1)S(1)}, bf16[3,5,16,16]{2,1,3,0:T(8,128)(2,1)S(1)}, u32[]{:S(2)}, u32[]{:S(2)}) collective-permute-start(bf16[3,5,16,16]{2,1,3,0:T(8,128)(2,1)S(1)} %copy.50), channel_id=1, source_target_pairs={{0,4},{4,8},{8,12},{1,5},{5,9},{9,13},{2,6},{6,10},{10,14},{3,7},{... | collective-permute-start | bytes 23048 | tf_op jit(solution)/shard_map/while/body/eval_jaxpr/ppermute | solution.py:16
  71.5 5.9 %collective-permute-start = (bf16[3,5,16,16]{2,1,3,0:T(8,128)(2,1)S(1)}, bf16[3,5,16,16]{2,1,3,0:T(8,128)(2,1)S(1)}, u32[]{:S(2)}, u32[]{:S(2)}) collective-permute-start(bf16[3,5,16,16]{2,1,3,0:T(8,128)(2,1)S(1)} %copy.50), channel_id=1, source_target_pairs={{0,4},{4,8},{8,12},{1,5},{5,9},{9,13},{2,6},{6,10},{10,14},{3,7},{... | collective-permute-start | bytes 23048 | tf_op jit(solution)/shard_map/while/body/eval_jaxpr/ppermute | solution.py:16
  105.7 5.9 %collective-permute-start = (bf16[3,5,16,16]{2,1,3,0:T(8,128)(2,1)S(1)}, bf16[3,5,16,16]{2,1,3,0:T(8,128)(2,1)S(1)}, u32[]{:S(2)}, u32[]{:S(2)}) collective-permute-start(bf16[3,5,16,16]{2,1,3,0:T(8,128)(2,1)S(1)} %copy.50), channel_id=1, source_target_pairs={{0,4},{4,8},{8,12},{1,5},{5,9},{9,13},{2,6},{6,10},{10,14},{3,7},{... | collective-permute-start | bytes 23048 | tf_op jit(solution)/shard_map/while/body/eval_jaxpr/ppermute | solution.py:16
where the time goes:
time: 142 us; the launch traced here: 141 us
  blocking collectives  59.4 us (42%)
  matrix products  42 us (30%)
  local copies, waits for them, and re-layouts  15.4 us (11%)
  waiting for transfers between devices  15.1 us (11%)
  starting transfers between devices  7.68 us (5%)
    all_gather x4, blocking collectives, chain_step(): full_front = lax.all_gather(previous, 'group', axis=3, tiled=True)  59.4 us
    dot_general x4, matrix products, solve_section(): result = jnp.einsum('eij,je->ie', inv_s, flat, precision=HIGH)  36.5 us
    ppermute x4, waiting for transfers between devices, passed_along(): lax.ppermute(value, axis, [(source, source + steps) for source in range(i...  15.1 us
    ppermute x4, starting transfers between devices, passed_along(): lax.ppermute(value, axis, [(source, source + steps) for source in range(i...  7.68 us
    gather x12, local copies, waits for them, and re-layouts, solve_section(): jnp.take(prev_full[k], up_s[k], axis=2)  6.88 us
    dot_general x4, matrix products, solve_section(): coupling = jnp.einsum('kif,kwfe->wie', lift, mixed, precision=HIGH)  4.27 us
    while x3, local copies, waits for them, and re-layouts, body(): ended, solution = lax.fori_loop(0, chains, chain_step, start)  2.94 us
  transfers between devices with their start and end apart: 4, of which 4 were waited for; matrix products, arithmetic and copies ran while one was open for 1% of the time, Pallas kernels for 0%

commit v1 on v0

--- a/solution.py
+++ b/solution.py
@@ -8,6 +8,18 @@
 NODES = 64
 FACE = 16
 HIGH = lax.Precision.HIGHEST
+
+
+def doubled_up(x, axis, dim):
+    ways, here = (lax.axis_size(axis), lax.axis_index(axis))
+    grown, reach = (x, 1)
+    while reach < ways:
+        theirs = lax.ppermute(grown, axis, [(d, d ^ reach) for d in range(ways)])
+        mine_first = jnp.concatenate([grown, theirs], axis=dim)
+        theirs_first = jnp.concatenate([theirs, grown], axis=dim)
+        grown = jnp.where(here & reach == 0, mine_first, theirs_first)
+        reach = 2 * reach
+    return grown
 
 
 def passed_along(value, axis, steps):
@@ -43,7 +55,7 @@
     def chain_step(turn, carry):
         last_traces, solved_all = carry
         previous = passed_along(last_traces, "chain", 1)
-        full_front = lax.all_gather(previous, "group", axis=3, tiled=True)
+        full_front = doubled_up(previous, "group", 3)
         solved = solve_section(rhs[0], inv_block[0], flux_jac[0], up_elem[0], full_front, lift)
         solved_list = [solved]
         previous = face_traces(solved)

time: 142 us -> 124 us (0.87)
  blocking collectives: 59.4 us -> 0 us
  starting transfers between devices: 7.68 us -> 27.5 us
  waiting for transfers between devices: 15.1 us -> 33.4 us
  local copies, waits for them, and re-layouts: 15.4 us -> 17 us
    all_gather x4 -> x0, blocking collectives: 59.4 us -> none  [chain_step(): full_front = lax.all_gather(previous, 'group', axis=3, tiled=True)]
    ppermute x0 -> x8, starting transfers between devices: none -> 19.8 us  [doubled_up(): theirs = lax.ppermute(grown, axis, [(d, d ^ reach) for d in range(ways)])]
    ppermute x0 -> x8, waiting for transfers between devices: none -> 19.1 us  [doubled_up(): theirs = lax.ppermute(grown, axis, [(d, d ^ reach) for d in range(ways)])]
    concatenate x0 -> x8, local copies, waits for them, and re-layouts: none -> 2.11 us  [the longest x4 1.06 us: doubled_up(): mine_first = jnp.concatenate([grown, theirs], axis=dim)]
  transfers between devices with their start and end apart: 4 -> 12, of which waited for: 4 -> 12; matrix products, arithmetic and copies ran while one was open for 1% -> 1% of each run, Pallas kernels for 0% -> 0%
where the time goes in v1:
time: 124 us; the launch traced here: 123 us
  matrix products  42 us (34%)
  waiting for transfers between devices  33.4 us (27%)
  starting transfers between devices  27.5 us (22%)
  local copies, waits for them, and re-layouts  17 us (14%)
  other arithmetic  2.02 us (2%)
    dot_general x4, matrix products, solve_section(): result = jnp.einsum('eij,je->ie', inv_s, flat, precision=HIGH)  36.5 us
    ppermute x8, starting transfers between devices, doubled_up(): theirs = lax.ppermute(grown, axis, [(d, d ^ reach) for d in range(ways)])  19.8 us
    ppermute x8, waiting for transfers between devices, doubled_up(): theirs = lax.ppermute(grown, axis, [(d, d ^ reach) for d in range(ways)])  19.1 us
    ppermute x4, waiting for transfers between devices, passed_along(): lax.ppermute(value, axis, [(source, source + steps) for source in range(i...  14.3 us
    ppermute x4, starting transfers between devices, passed_along(): lax.ppermute(value, axis, [(source, source + steps) for source in range(i...  7.68 us
    gather x12, local copies, waits for them, and re-layouts, solve_section(): jnp.take(prev_full[k], up_s[k], axis=2)  6.88 us
    dot_general x4, matrix products, solve_section(): coupling = jnp.einsum('kif,kwfe->wie', lift, mixed, precision=HIGH)  4.28 us
    while x3, local copies, waits for them, and re-layouts, body(): ended, solution = lax.fori_loop(0, chains, chain_step, start)  2.94 us
  transfers between devices with their start and end apart: 12, of which 12 were waited for; matrix products, arithmetic and copies ran while one was open for 1% of the time, Pallas kernels for 0%

profile of v1, /device:TPU:6, one launch (start us, length us, event | category | flops | bytes accessed | tf_op | source)
XLA Modules:
  0.0 122.6 jit_solution(3523454253051232136)
XLA Ops:
  0.0 0.8 copy.31
  0.8 0.7 copy.30
  1.5 119.7 %while.12 = (s32[]{:T(128)}, bf16[3,5,16,16]{3,2,1,0:T(8,128)(2,1)S(1)}, f32[1,5,64,16]{2,1,3,0:T(8,128)}, f32[1,5,64,16]{2,3,1,0:T(8,128)}, s32[1,3,16]{2,1,0:T...) while((s32[]{:T(128)}, ...), condition=%wide.region_1.3_spmd, body=%wide.region_0.2_spmd.sunk | while | flops 23075368 | bytes 7497421 | solution.py:65
  1.5 1.9 %collective-permute-start = (bf16[3,5,16,16]{3,2,1,0:T(8,128)(2,1)S(1)}, bf16[3,5,16,16]{3,2,1,0:T(8,128)(2,1)S(1)}, u32[]{:S(2)}, u32[]{:S(2)}) collective-permute-start(bf16[3,5,16,16]{3,2,1,0:T(8,128)(2,1)S(1)} %get-tuple-element.199), channel_id=1, source_target_pairs={{0,4},{4,8},{8,12},{1,5},{5,9},{9,13},{2,6},{6,10},{10,14},{3,7},{... | collective-permute-start | bytes 23048 | tf_op jit(solution)/shard_map/while/body/eval_jaxpr/ppermute | solution.py:28
  3.5 3.6 %collective-permute-done = bf16[3,5,16,16]{3,2,1,0:T(8,128)(2,1)S(1)} collective-permute-done((bf16[3,5,16,16]{3,2,1,0:T(8,128)(2,1)S(1)}, bf16[3,5,16,16]{3,2,1,0:T(8,128)(2,1)S(1)}, u32[]{:S(2)}, u32[]{:S(2)}) %collective-permute-start) | collective-permute-done | bytes 7712 | tf_op jit(solution)/shard_map/while/body/eval_jaxpr/ppermute | solution.py:28
  7.0 1.6 %collective-permute-start.1 = (bf16[3,5,16,16]{3,2,1,0:T(8,128)(2,1)S(1)}, bf16[3,5,16,16]{3,2,1,0:T(8,128)(2,1)S(1)}, u32[]{:S(2)}, u32[]{:S(2)}) collective-permute-start(bf16[3,5,16,16]{3,2,1,0:T(8,128)(2,1)S(1)} %collective-permute-done), channel_id=1, source_target_pairs={{0,1},{1,0},{2,3},{3,2},{4,5},{5,4},{6,7},{7,6},{8,9},{9,8},{10,11... | collective-permute-start | bytes 23048 | tf_op jit(solution)/shard_map/while/body/eval_jaxpr/ppermute | solution.py:17
  8.6 2.6 %collective-permute-done.1 = bf16[3,5,16,16]{3,2,1,0:T(8,128)(2,1)S(1)} collective-permute-done((bf16[3,5,16,16]{3,2,1,0:T(8,128)(2,1)S(1)}, bf16[3,5,16,16]{3,2,1,0:T(8,128)(2,1)S(1)}, u32[]{:S(2)}, u32[]{:S(2)}) %collective-permute-start.1) | collective-permute-done | bytes 7712 | tf_op jit(solution)/shard_map/while/body/eval_jaxpr/ppermute | solution.py:17
  11.4 3.1 %collective-permute-start.2 = (bf16[3,5,16,32]{3,2,1,0:T(8,128)(2,1)S(1)}, bf16[3,5,16,32]{3,2,1,0:T(8,128)(2,1)S(1)}, u32[]{:S(2)}, u32[]{:S(2)}) collective-permute-start(bf16[3,5,16,32]{3,2,1,0:T(8,128)(2,1)S(1)} %maximum_select_fusion.2), channel_id=1, source_target_pairs={{0,2},{1,3},{2,0},{3,1},{4,6},{5,7},{6,4},{7,5},{8,10},{9,11},{10,... | collective-permute-start | bytes 46088 | tf_op jit(solution)/shard_map/while/body/eval_jaxpr/ppermute | solution.py:17
  14.7 2.0 %collective-permute-done.2 = bf16[3,5,16,32]{3,2,1,0:T(8,128)(2,1)S(1)} collective-permute-done((bf16[3,5,16,32]{3,2,1,0:T(8,128)(2,1)S(1)}, bf16[3,5,16,32]{3,2,1,0:T(8,128)(2,1)S(1)}, u32[]{:S(2)}, u32[]{:S(2)}) %collective-permute-start.2) | collective-permute-done | bytes 15392 | tf_op jit(solution)/shard_map/while/body/eval_jaxpr/ppermute | solution.py:17
  16.8 0.3 copy.52
  17.1 0.3 copy.53
  17.5 0.6 gather_fusion.1
  18.0 0.6 gather_fusion
  18.6 0.6 gather_fusion.2
  19.4 0.3 convolution_bitcast_fusion.3
  19.7 1.1 fusion.27
  20.9 9.1 %fusion.28 = f32[16,1,320]{2,1,0:T(1,128)S(1)} fusion(f32[320,16,1]{0,2,1:T(1,128)S(1)} %reshape.74, f32[1,16,320,320]{3,2,1,0:T(8,128)} %get-tuple-element.217), kind=kOutput, calls=%fused_computation.3.clone.1 | convolution fusion | flops 19660800 | bytes 6594560 | tf_op jit(solution)/shard_map/while/body/eval_jaxpr/eij,je->ie/dot_general | solution.py:47
  30.3 0.7 reshape.75
  31.0 1.9 %collective-permute-start = (bf16[3,5,16,16]{3,2,1,0:T(8,128)(2,1)S(1)}, bf16[3,5,16,16]{3,2,1,0:T(8,128)(2,1)S(1)}, u32[]{:S(2)}, u32[]{:S(2)}) collective-permute-start(bf16[3,5,16,16]{3,2,1,0:T(8,128)(2,1)S(1)} %get-tuple-element.199), channel_id=1, source_target_pairs={{0,4},{4,8},{8,12},{1,5},{5,9},{9,13},{2,6},{6,10},{10,14},{3,7},{... | collective-permute-start | bytes 23048 | tf_op jit(solution)/shard_map/while/body/eval_jaxpr/ppermute | solution.py:28
  33.0 3.6 %collective-permute-done = bf16[3,5,16,16]{3,2,1,0:T(8,128)(2,1)S(1)} collective-permute-done((bf16[3,5,16,16]{3,2,1,0:T(8,128)(2,1)S(1)}, bf16[3,5,16,16]{3,2,1,0:T(8,128)(2,1)S(1)}, u32[]{:S(2)}, u32[]{:S(2)}) %collective-permute-start) | collective-permute-done | bytes 7712 | tf_op jit(solution)/shard_map/while/body/eval_jaxpr/ppermute | solution.py:28
  36.6 1.5 %collective-permute-start.1 = (bf16[3,5,16,16]{3,2,1,0:T(8,128)(2,1)S(1)}, bf16[3,5,16,16]{3,2,1,0:T(8,128)(2,1)S(1)}, u32[]{:S(2)}, u32[]{:S(2)}) collective-permute-start(bf16[3,5,16,16]{3,2,1,0:T(8,128)(2,1)S(1)} %collective-permute-done), channel_id=1, source_target_pairs={{0,1},{1,0},{2,3},{3,2},{4,5},{5,4},{6,7},{7,6},{8,9},{9,8},{10,11... | collective-permute-start | bytes 23048 | tf_op jit(solution)/shard_map/while/body/eval_jaxpr/ppermute | solution.py:17
  38.0 2.7 %collective-permute-done.1 = bf16[3,5,16,16]{3,2,1,0:T(8,128)(2,1)S(1)} collective-permute-done((bf16[3,5,16,16]{3,2,1,0:T(8,128)(2,1)S(1)}, bf16[3,5,16,16]{3,2,1,0:T(8,128)(2,1)S(1)}, u32[]{:S(2)}, u32[]{:S(2)}) %collective-permute-start.1) | collective-permute-done | bytes 7712 | tf_op jit(solution)/shard_map/while/body/eval_jaxpr/ppermute | solution.py:17
  40.9 3.6 %collective-permute-start.2 = (bf16[3,5,16,32]{3,2,1,0:T(8,128)(2,1)S(1)}, bf16[3,5,16,32]{3,2,1,0:T(8,128)(2,1)S(1)}, u32[]{:S(2)}, u32[]{:S(2)}) collective-permute-start(bf16[3,5,16,32]{3,2,1,0:T(8,128)(2,1)S(1)} %maximum_select_fusion.2), channel_id=1, source_target_pairs={{0,2},{1,3},{2,0},{3,1},{4,6},{5,7},{6,4},{7,5},{8,10},{9,11},{10,... | collective-permute-start | bytes 46088 | tf_op jit(solution)/shard_map/while/body/eval_jaxpr/ppermute | solution.py:17
  44.7 2.0 %collective-permute-done.2 = bf16[3,5,16,32]{3,2,1,0:T(8,128)(2,1)S(1)} collective-permute-done((bf16[3,5,16,32]{3,2,1,0:T(8,128)(2,1)S(1)}, bf16[3,5,16,32]{3,2,1,0:T(8,128)(2,1)S(1)}, u32[]{:S(2)}, u32[]{:S(2)}) %collective-permute-start.2) | collective-permute-done | bytes 15392 | tf_op jit(solution)/shard_map/while/body/eval_jaxpr/ppermute | solution.py:17
  46.8 0.3 copy.52
  47.1 0.3 copy.53
  47.5 0.6 gather_fusion.1
  48.1 0.6 gather_fusion
  48.6 0.6 gather_fusion.2
  49.4 0.3 convolution_bitcast_fusion.3
  49.7 1.1 fusion.27
  50.9 9.1 %fusion.28 = f32[16,1,320]{2,1,0:T(1,128)S(1)} fusion(f32[320,16,1]{0,2,1:T(1,128)S(1)} %reshape.74, f32[1,16,320,320]{3,2,1,0:T(8,128)} %get-tuple-element.217), kind=kOutput, calls=%fused_computation.3.clone.1 | convolution fusion | flops 19660800 | bytes 6594560 | tf_op jit(solution)/shard_map/while/body/eval_jaxpr/eij,je->ie/dot_general | solution.py:47
  60.3 0.7 reshape.75
  61.0 1.9 %collective-permute-start = (bf16[3,5,16,16]{3,2,1,0:T(8,128)(2,1)S(1)}, bf16[3,5,16,16]{3,2,1,0:T(8,128)(2,1)S(1)}, u32[]{:S(2)}, u32[]{:S(2)}) collective-permute-start(bf16[3,5,16,16]{3,2,1,0:T(8,128)(2,1)S(1)} %get-tuple-element.199), channel_id=1, source_target_pairs={{0,4},{4,8},{8,12},{1,5},{5,9},{9,13},{2,6},{6,10},{10,14},{3,7},{... | collective-permute-start | bytes 23048 | tf_op jit(solution)/shard_map/while/body/eval_jaxpr/ppermute | solution.py:28
  63.0 3.6 %collective-permute-done = bf16[3,5,16,16]{3,2,1,0:T(8,128)(2,1)S(1)} collective-permute-done((bf16[3,5,16,16]{3,2,1,0:T(8,128)(2,1)S(1)}, bf16[3,5,16,16]{3,2,1,0:T(8,128)(2,1)S(1)}, u32[]{:S(2)}, u32[]{:S(2)}) %collective-permute-start) | collective-permute-done | bytes 7712 | tf_op jit(solution)/shard_map/while/body/eval_jaxpr/ppermute | solution.py:28
  66.6 1.4 %collective-permute-start.1 = (bf16[3,5,16,16]{3,2,1,0:T(8,128)(2,1)S(1)}, bf16[3,5,16,16]{3,2,1,0:T(8,128)(2,1)S(1)}, u32[]{:S(2)}, u32[]{:S(2)}) collective-permute-start(bf16[3,5,16,16]{3,2,1,0:T(8,128)(2,1)S(1)} %collective-permute-done), channel_id=1, source_target_pairs={{0,1},{1,0},{2,3},{3,2},{4,5},{5,4},{6,7},{7,6},{8,9},{9,8},{10,11... | collective-permute-start | bytes 23048 | tf_op jit(solution)/shard_map/while/body/eval_jaxpr/ppermute | solution.py:17
  68.0 2.8 %collective-permute-done.1 = bf16[3,5,16,16]{3,2,1,0:T(8,128)(2,1)S(1)} collective-permute-done((bf16[3,5,16,16]{3,2,1,0:T(8,128)(2,1)S(1)}, bf16[3,5,16,16]{3,2,1,0:T(8,128)(2,1)S(1)}, u32[]{:S(2)}, u32[]{:S(2)}) %collective-permute-start.1) | collective-permute-done | bytes 7712 | tf_op jit(solution)/shard_map/while/body/eval_jaxpr/ppermute | solution.py:17
  70.9 3.6 %collective-permute-start.2 = (bf16[3,5,16,32]{3,2,1,0:T(8,128)(2,1)S(1)}, bf16[3,5,16,32]{3,2,1,0:T(8,128)(2,1)S(1)}, u32[]{:S(2)}, u32[]{:S(2)}) collective-permute-start(bf16[3,5,16,32]{3,2,1,0:T(8,128)(2,1)S(1)} %maximum_select_fusion.2), channel_id=1, source_target_pairs={{0,2},{1,3},{2,0},{3,1},{4,6},{5,7},{6,4},{7,5},{8,10},{9,11},{10,... | collective-permute-start | bytes 46088 | tf_op jit(solution)/shard_map/while/body/eval_jaxpr/ppermute | solution.py:17
  74.7 2.0 %collective-permute-done.2 = bf16[3,5,16,32]{3,2,1,0:T(8,128)(2,1)S(1)} collective-permute-done((bf16[3,5,16,32]{3,2,1,0:T(8,128)(2,1)S(1)}, bf16[3,5,16,32]{3,2,1,0:T(8,128)(2,1)S(1)}, u32[]{:S(2)}, u32[]{:S(2)}) %collective-permute-start.2) | collective-permute-done | bytes 15392 | tf_op jit(solution)/shard_map/while/body/eval_jaxpr/ppermute | solution.py:17
  76.9 0.3 copy.52
  77.1 0.3 copy.53
  77.5 0.6 gather_fusion.1
  78.1 0.6 gather_fusion
  78.7 0.6 gather_fusion.2
  79.5 0.3 convolution_bitcast_fusion.3
  79.8 1.1 fusion.27
  81.0 9.1 %fusion.28 = f32[16,1,320]{2,1,0:T(1,128)S(1)} fusion(f32[320,16,1]{0,2,1:T(1,128)S(1)} %reshape.74, f32[1,16,320,320]{3,2,1,0:T(8,128)} %get-tuple-element.217), kind=kOutput, calls=%fused_computation.3.clone.1 | convolution fusion | flops 19660800 | bytes 6594560 | tf_op jit(solution)/shard_map/while/body/eval_jaxpr/eij,je->ie/dot_general | solution.py:47
  90.4 0.7 reshape.75
  91.1 1.9 %collective-permute-start = (bf16[3,5,16,16]{3,2,1,0:T(8,128)(2,1)S(1)}, bf16[3,5,16,16]{3,2,1,0:T(8,128)(2,1)S(1)}, u32[]{:S(2)}, u32[]{:S(2)}) collective-permute-start(bf16[3,5,16,16]{3,2,1,0:T(8,128)(2,1)S(1)} %get-tuple-element.199), channel_id=1, source_target_pairs={{0,4},{4,8},{8,12},{1,5},{5,9},{9,13},{2,6},{6,10},{10,14},{3,7},{... | collective-permute-start | bytes 23048 | tf_op jit(solution)/shard_map/while/body/eval_jaxpr/ppermute | solution.py:28
  93.1 3.6 %collective-permute-done = bf16[3,5,16,16]{3,2,1,0:T(8,128)(2,1)S(1)} collective-permute-done((bf16[3,5,16,16]{3,2,1,0:T(8,128)(2,1)S(1)}, bf16[3,5,16,16]{3,2,1,0:T(8,128)(2,1)S(1)}, u32[]{:S(2)}, u32[]{:S(2)}) %collective-permute-start) | collective-permute-done | bytes 7712 | tf_op jit(solution)/shard_map/while/body/eval_jaxpr/ppermute | solution.py:28
  96.6 1.4 %collective-permute-start.1 = (bf16[3,5,16,16]{3,2,1,0:T(8,128)(2,1)S(1)}, bf16[3,5,16,16]{3,2,1,0:T(8,128)(2,1)S(1)}, u32[]{:S(2)}, u32[]{:S(2)}) collective-permute-start(bf16[3,5,16,16]{3,2,1,0:T(8,128)(2,1)S(1)} %collective-permute-done), channel_id=1, source_target_pairs={{0,1},{1,0},{2,3},{3,2},{4,5},{5,4},{6,7},{7,6},{8,9},{9,8},{10,11... | collective-permute-start | bytes 23048 | tf_op jit(solution)/shard_map/while/body/eval_jaxpr/ppermute | solution.py:17
  98.0 2.8 %collective-permute-done.1 = bf16[3,5,16,16]{3,2,1,0:T(8,128)(2,1)S(1)} collective-permute-done((bf16[3,5,16,16]{3,2,1,0:T(8,128)(2,1)S(1)}, bf16[3,5,16,16]{3,2,1,0:T(8,128)(2,1)S(1)}, u32[]{:S(2)}, u32[]{:S(2)}) %collective-permute-start.1) | collective-permute-done | bytes 7712 | tf_op jit(solution)/shard_map/while/body/eval_jaxpr/ppermute | solution.py:17
  101.0 3.6 %collective-permute-start.2 = (bf16[3,5,16,32]{3,2,1,0:T(8,128)(2,1)S(1)}, bf16[3,5,16,32]{3,2,1,0:T(8,128)(2,1)S(1)}, u32[]{:S(2)}, u32[]{:S(2)}) collective-permute-start(bf16[3,5,16,32]{3,2,1,0:T(8,128)(2,1)S(1)} %maximum_select_fusion.2), channel_id=1, source_target_pairs={{0,2},{1,3},{2,0},{3,1},{4,6},{5,7},{6,4},{7,5},{8,10},{9,11},{10,... | collective-permute-start | bytes 46088 | tf_op jit(solution)/shard_map/while/body/eval_jaxpr/ppermute | solution.py:17
  104.8 2.0 %collective-permute-done.2 = bf16[3,5,16,32]{3,2,1,0:T(8,128)(2,1)S(1)} collective-permute-done((bf16[3,5,16,32]{3,2,1,0:T(8,128)(2,1)S(1)}, bf16[3,5,16,32]{3,2,1,0:T(8,128)(2,1)S(1)}, u32[]{:S(2)}, u32[]{:S(2)}) %collective-permute-start.2) | collective-permute-done | bytes 15392 | tf_op jit(solution)/shard_map/while/body/eval_jaxpr/ppermute | solution.py:17
  106.9 0.3 copy.52
  107.2 0.3 copy.53
  107.6 0.6 gather_fusion.1
  108.2 0.6 gather_fusion
  108.8 0.6 gather_fusion.2
  109.5 0.3 convolution_bitcast_fusion.3
  109.8 1.1 fusion.27
  111.0 9.1 %fusion.28 = f32[16,1,320]{2,1,0:T(1,128)S(1)} fusion(f32[320,16,1]{0,2,1:T(1,128)S(1)} %reshape.74, f32[1,16,320,320]{3,2,1,0:T(8,128)} %get-tuple-element.217), kind=kOutput, calls=%fused_computation.3.clone.1 | convolution fusion | flops 19660800 | bytes 6594560 | tf_op jit(solution)/shard_map/while/body/eval_jaxpr/eij,je->ie/dot_general | solution.py:47
  120.4 0.7 reshape.75
  121.1 1.5 %copy.32 = f32[1,5,64,16]{2,3,1,0:T(8,128)} copy(f32[1,5,64,16]{2,1,3,0:T(8,128)} %get-tuple-element.47) | data formatting | bytes 40960 | tf_op jit(solution)/shard_map/while | solution.py:65
  (82 shorter events, 4.3 us)
Async XLA Ops:
  1.5 5.5 %collective-permute-start = (bf16[3,5,16,16]{3,2,1,0:T(8,128)(2,1)S(1)}, bf16[3,5,16,16]{3,2,1,0:T(8,128)(2,1)S(1)}, u32[]{:S(2)}, u32[]{:S(2)}) collective-permute-start(bf16[3,5,16,16]{3,2,1,0:T(8,128)(2,1)S(1)} %get-tuple-element.199), channel_id=1, source_target_pairs={{0,4},{4,8},{8,12},{1,5},{5,9},{9,13},{2,6},{6,10},{10,14},{3,7},{... | collective-permute-start | bytes 23048 | tf_op jit(solution)/shard_map/while/body/eval_jaxpr/ppermute | solution.py:28
  7.0 4.2 %collective-permute-start.1 = (bf16[3,5,16,16]{3,2,1,0:T(8,128)(2,1)S(1)}, bf16[3,5,16,16]{3,2,1,0:T(8,128)(2,1)S(1)}, u32[]{:S(2)}, u32[]{:S(2)}) collective-permute-start(bf16[3,5,16,16]{3,2,1,0:T(8,128)(2,1)S(1)} %collective-permute-done), channel_id=1, source_target_pairs={{0,1},{1,0},{2,3},{3,2},{4,5},{5,4},{6,7},{7,6},{8,9},{9,8},{10,11... | collective-permute-start | bytes 23048 | tf_op jit(solution)/shard_map/while/body/eval_jaxpr/ppermute | solution.py:17
  11.4 5.3 %collective-permute-start.2 = (bf16[3,5,16,32]{3,2,1,0:T(8,128)(2,1)S(1)}, bf16[3,5,16,32]{3,2,1,0:T(8,128)(2,1)S(1)}, u32[]{:S(2)}, u32[]{:S(2)}) collective-permute-start(bf16[3,5,16,32]{3,2,1,0:T(8,128)(2,1)S(1)} %maximum_select_fusion.2), channel_id=1, source_target_pairs={{0,2},{1,3},{2,0},{3,1},{4,6},{5,7},{6,4},{7,5},{8,10},{9,11},{10,... | collective-permute-start | bytes 46088 | tf_op jit(solution)/shard_map/while/body/eval_jaxpr/ppermute | solution.py:17
  31.0 5.5 %collective-permute-start = (bf16[3,5,16,16]{3,2,1,0:T(8,128)(2,1)S(1)}, bf16[3,5,16,16]{3,2,1,0:T(8,128)(2,1)S(1)}, u32[]{:S(2)}, u32[]{:S(2)}) collective-permute-start(bf16[3,5,16,16]{3,2,1,0:T(8,128)(2,1)S(1)} %get-tuple-element.199), channel_id=1, source_target_pairs={{0,4},{4,8},{8,12},{1,5},{5,9},{9,13},{2,6},{6,10},{10,14},{3,7},{... | collective-permute-start | bytes 23048 | tf_op jit(solution)/shard_map/while/body/eval_jaxpr/ppermute | solution.py:28
  36.6 4.2 %collective-permute-start.1 = (bf16[3,5,16,16]{3,2,1,0:T(8,128)(2,1)S(1)}, bf16[3,5,16,16]{3,2,1,0:T(8,128)(2,1)S(1)}, u32[]{:S(2)}, u32[]{:S(2)}) collective-permute-start(bf16[3,5,16,16]{3,2,1,0:T(8,128)(2,1)S(1)} %collective-permute-done), channel_id=1, source_target_pairs={{0,1},{1,0},{2,3},{3,2},{4,5},{5,4},{6,7},{7,6},{8,9},{9,8},{10,11... | collective-permute-start | bytes 23048 | tf_op jit(solution)/shard_map/while/body/eval_jaxpr/ppermute | solution.py:17
  40.9 5.8 %collective-permute-start.2 = (bf16[3,5,16,32]{3,2,1,0:T(8,128)(2,1)S(1)}, bf16[3,5,16,32]{3,2,1,0:T(8,128)(2,1)S(1)}, u32[]{:S(2)}, u32[]{:S(2)}) collective-permute-start(bf16[3,5,16,32]{3,2,1,0:T(8,128)(2,1)S(1)} %maximum_select_fusion.2), channel_id=1, source_target_pairs={{0,2},{1,3},{2,0},{3,1},{4,6},{5,7},{6,4},{7,5},{8,10},{9,11},{10,... | collective-permute-start | bytes 46088 | tf_op jit(solution)/shard_map/while/body/eval_jaxpr/ppermute | solution.py:17
  61.0 5.5 %collective-permute-start = (bf16[3,5,16,16]{3,2,1,0:T(8,128)(2,1)S(1)}, bf16[3,5,16,16]{3,2,1,0:T(8,128)(2,1)S(1)}, u32[]{:S(2)}, u32[]{:S(2)}) collective-permute-start(bf16[3,5,16,16]{3,2,1,0:T(8,128)(2,1)S(1)} %get-tuple-element.199), channel_id=1, source_target_pairs={{0,4},{4,8},{8,12},{1,5},{5,9},{9,13},{2,6},{6,10},{10,14},{3,7},{... | collective-permute-start | bytes 23048 | tf_op jit(solution)/shard_map/while/body/eval_jaxpr/ppermute | solution.py:28
  66.6 4.2 %collective-permute-start.1 = (bf16[3,5,16,16]{3,2,1,0:T(8,128)(2,1)S(1)}, bf16[3,5,16,16]{3,2,1,0:T(8,128)(2,1)S(1)}, u32[]{:S(2)}, u32[]{:S(2)}) collective-permute-start(bf16[3,5,16,16]{3,2,1,0:T(8,128)(2,1)S(1)} %collective-permute-done), channel_id=1, source_target_pairs={{0,1},{1,0},{2,3},{3,2},{4,5},{5,4},{6,7},{7,6},{8,9},{9,8},{10,11... | collective-permute-start | bytes 23048 | tf_op jit(solution)/shard_map/while/body/eval_jaxpr/ppermute | solution.py:17
  70.9 5.8 %collective-permute-start.2 = (bf16[3,5,16,32]{3,2,1,0:T(8,128)(2,1)S(1)}, bf16[3,5,16,32]{3,2,1,0:T(8,128)(2,1)S(1)}, u32[]{:S(2)}, u32[]{:S(2)}) collective-permute-start(bf16[3,5,16,32]{3,2,1,0:T(8,128)(2,1)S(1)} %maximum_select_fusion.2), channel_id=1, source_target_pairs={{0,2},{1,3},{2,0},{3,1},{4,6},{5,7},{6,4},{7,5},{8,10},{9,11},{10,... | collective-permute-start | bytes 46088 | tf_op jit(solution)/shard_map/while/body/eval_jaxpr/ppermute | solution.py:17
  91.1 5.5 %collective-permute-start = (bf16[3,5,16,16]{3,2,1,0:T(8,128)(2,1)S(1)}, bf16[3,5,16,16]{3,2,1,0:T(8,128)(2,1)S(1)}, u32[]{:S(2)}, u32[]{:S(2)}) collective-permute-start(bf16[3,5,16,16]{3,2,1,0:T(8,128)(2,1)S(1)} %get-tuple-element.199), channel_id=1, source_target_pairs={{0,4},{4,8},{8,12},{1,5},{5,9},{9,13},{2,6},{6,10},{10,14},{3,7},{... | collective-permute-start | bytes 23048 | tf_op jit(solution)/shard_map/while/body/eval_jaxpr/ppermute | solution.py:28
  96.6 4.2 %collective-permute-start.1 = (bf16[3,5,16,16]{3,2,1,0:T(8,128)(2,1)S(1)}, bf16[3,5,16,16]{3,2,1,0:T(8,128)(2,1)S(1)}, u32[]{:S(2)}, u32[]{:S(2)}) collective-permute-start(bf16[3,5,16,16]{3,2,1,0:T(8,128)(2,1)S(1)} %collective-permute-done), channel_id=1, source_target_pairs={{0,1},{1,0},{2,3},{3,2},{4,5},{5,4},{6,7},{7,6},{8,9},{9,8},{10,11... | collective-permute-start | bytes 23048 | tf_op jit(solution)/shard_map/while/body/eval_jaxpr/ppermute | solution.py:17
  101.0 5.8 %collective-permute-start.2 = (bf16[3,5,16,32]{3,2,1,0:T(8,128)(2,1)S(1)}, bf16[3,5,16,32]{3,2,1,0:T(8,128)(2,1)S(1)}, u32[]{:S(2)}, u32[]{:S(2)}) collective-permute-start(bf16[3,5,16,32]{3,2,1,0:T(8,128)(2,1)S(1)} %maximum_select_fusion.2), channel_id=1, source_target_pairs={{0,2},{1,3},{2,0},{3,1},{4,6},{5,7},{6,4},{7,5},{8,10},{9,11},{10,... | collective-permute-start | bytes 46088 | tf_op jit(solution)/shard_map/while/body/eval_jaxpr/ppermute | solution.py:17
